TPU v7x, 128 devices: a whole 4x4x4 slice. The times are simulated.
128 devices in a mesh: row: 16 (over z_lo, x, core), col: 8 (over y, z_hi).
Axes of the slice: x: 4, y: 4, z: 4 (z_hi: 2, z_lo: 2; z = z_hi * 2 + z_lo), core: 2. Of those that a mesh axis runs over, the one named last changes fastest.
Arguments:
- shared_rows: float32 [2048, 16384], P('row', 'col'), may hold values from -0.125 to 0.125
- event_counts: int32 [16], replicated, may hold values from 32 to 128, as said below
- ridge: float32 [16384], P('col'), may hold values from 0.5 to 2
- items: float32 [1024, 16384], P('row', 'col'), may hold values from -6 to 6
- cand_ids: int32 [512], replicated, may hold values from 0 to 1023
- theta: float32 [16384], P('col'), may hold values from -0.046875 to 0.046875
Outputs:
- gram_tile: float32 [16384, 16384], P('row', 'col')
- scores: float32 [512], replicated
Inputs may be any that keep to these rules, and one draw needn't show every extreme that they name: event_counts[s] counts the live slots at the start of row shard s's 128 slots; some shard is full.
All inputs are finite; a program needn't handle non-finite values.
Results may differ from a plain program's by a relative error of at most 0.000068.
Values sent between devices are 32-bit elements; how exact they have to be, the bound alone decides.
No kernel may reach another device: no remote copies, remote signals or barrier semaphores. Data moves between devices by JAX's collectives and lax.ppermute only.
A program may use at most 128 MiB of HBM per device.

v0:
```python
import jax
import jax.numpy as jnp
from jax import lax
from jax.sharding import PartitionSpec as P

F = 16384
high = lax.Precision.HIGHEST


def spread(value, axis, source):
    kept = jnp.where(lax.axis_index(axis) == source, value, 0).astype(value.dtype)
    return lax.psum(kept, axis)


def body(shared_rows, event_counts, ridge, items, cand_ids, theta):
    ratio = lax.axis_size("row") // lax.axis_size("col")
    row_pos = lax.axis_index("row")
    col_pos = lax.axis_index("col")
    width_col = shared_rows.shape[1]
    width_row = width_col // ratio
    ev_slots = shared_rows.shape[0]
    slot = lax.iota(jnp.int32, ev_slots)
    masked = jnp.where((slot < event_counts[row_pos])[:, None], shared_rows, jnp.float32(0.0))
    offset = row_pos % ratio * width_row
    root = row_pos // ratio
    contract = (((0,), (0,)), ((), ()))
    col_all = lax.all_gather(masked, "row", axis=0, tiled=True)
    row_all = spread(lax.dynamic_slice_in_dim(col_all, offset, width_row, 1), "col", root)
    tile = lax.dot_general(
        row_all, col_all, contract, precision=high, preferred_element_type=jnp.float32
    )
    rows_global = row_pos * width_row + lax.broadcasted_iota(jnp.int32, (width_row, width_col), 0)
    cols_global = col_pos * width_col + lax.broadcasted_iota(jnp.int32, (width_row, width_col), 1)
    tile = tile + jnp.where(rows_global == cols_global, ridge[None, :], jnp.float32(0.0))
    items_dev = items.shape[0]
    onehot = (
        cand_ids[:, None] == row_pos * items_dev + lax.iota(jnp.int32, items_dev)[None, :]
    ).astype(jnp.float32)
    picked = jnp.dot(onehot, items, precision=high, preferred_element_type=jnp.float32)
    cand_col = lax.psum(picked, "row")
    across = (((1,), (1,)), ((), ()))
    cand_row = spread(lax.dynamic_slice_in_dim(cand_col, offset, width_row, 1), "col", root)
    image_part = lax.dot_general(
        cand_col, tile, across, precision=high, preferred_element_type=jnp.float32
    )
    image_row = lax.psum(image_part, "col")
    quad = jnp.where(col_pos == 0, jnp.sum(cand_row * image_row, axis=1), jnp.float32(0.0))
    linear = jnp.where(
        row_pos == 0,
        jnp.dot(cand_col, theta, precision=high, preferred_element_type=jnp.float32),
        jnp.float32(0.0),
    )
    quad_all, linear_all = lax.psum((quad, linear), ("row", "col"))
    return (tile, linear_all + jnp.sqrt(quad_all / F))


def solution(mesh):
    return jax.shard_map(
        body,
        mesh=mesh,
        in_specs=(P("row", "col"), P(), P("col"), P("row", "col"), P(), P("col")),
        out_specs=(P("row", "col"), P()),
        check_vma=False,
    )
```

profile of v0, /device:TPU:1, one launch (start us, length us, event | category | flops | bytes accessed | tf_op | source)
XLA Modules:
  0.0 940.3 jit_solution(5957106584917055528)
XLA Ops:
  7.2 0.0 copy-start
  7.2 0.0 all-gather.2.cloned.1.call-start
  7.2 1.3 dynamic_slice.9
  8.5 0.6 iota_compare_fusion
  9.2 2.3 broadcast_select_fusion
  11.5 0.0 all-gather.2.cloned.1.call-update
  11.5 0.0 all-reduce.8.cloned.1.call-start
  11.6 0.0 copy-done
  11.6 4.5 fusion
  16.1 0.0 all-reduce.8.cloned.1.call-update
  16.1 0.0 all-reduce.6.cloned.1.call-start
  16.2 90.8 %all-gather.2.cloned.1.call-done = f32[2048,2048]{1,0:T(8,128)} async-done(((f32[128,2048]{1,0:T(8,128)}), f32[2048,2048]{1,0:T(8,128)}) %all-gather.2.cloned.1.call-update) | async-done | bytes 16777232 | tf_op jit(solution)/shard_map/all_gather | solution.py:27
  107.0 8.7 dynamic-slice_select_fusion
  115.7 0.0 copy-start.3
  115.7 0.0 all-reduce.6.cloned.1.call-update
  115.7 0.0 all-reduce.10.cloned.1.call-start
  115.8 122.9 %all-reduce.8.cloned.1.call-done = f32[512,2048]{1,0:T(8,128)} async-done(((f32[512,2048]{1,0:T(8,128)}), f32[512,2048]{1,0:T(8,128)}) %all-reduce.8.cloned.1.call-update) | async-done | bytes 4194320 | tf_op jit(solution)/shard_map/psum | solution.py:40
  238.7 3.2 dynamic-slice_select_fusion.1
  241.9 343.4 %all-reduce.6.cloned.1.call-done = f32[2048,1024]{1,0:T(8,128)} async-done(((f32[2048,1024]{1,0:T(8,128)}), f32[2048,1024]{1,0:T(8,128)}) %all-reduce.6.cloned.1.call-update) | async-done | bytes 8388624 | tf_op jit(solution)/shard_map/psum | solution.py:12
  585.3 0.0 copy-done.3
  585.3 0.0 copy-start.1
  585.3 67.7 %select_add_fusion = f32[1024,2048]{1,0:T(8,128)S(1)} fusion(f32[2048]{0:T(1024)S(1)} %copy-done.3, s32[2048]{0:T(1024)S(1)} %iota_add_fusion, s32[1024]{0:T(1024)S(1)} %iota_add_fusion.1, f32[2048,1024]{1,0:T(8,128)} %all-reduce.6.cloned.1.call-done, f32[2048,2048]{1,0:T(8,128)} %all-gather.2.cloned.1.call-done), kind=kOutput, calls=%fused_computation | convolution fusion | flops 51545899008 | bytes 33574912 | tf_op jit(solution)/shard_map/dot_general | solution.py:29
  653.1 0.0 copy-start.4
  653.1 3.4 copy-done.4
  656.5 0.0 copy-done.1
  656.5 0.0 copy-start.2
  656.5 15.2 %fusion.5 = f32[512,1024]{1,0:T(8,128)} fusion(f32[512,2048]{1,0:T(8,128)S(1)} %copy-done.1, f32[1024,2048]{1,0:T(8,128)S(1)} %select_add_fusion), kind=kOutput, calls=%fused_computation.17 | convolution fusion | flops 12884901888 | bytes 14680064 | tf_op jit(solution)/shard_map/dot_general | solution.py:43
  671.7 0.0 all-reduce.10.cloned.1.call-update
  671.7 0.0 copy-done.2
  671.7 5.8 fusion.4
  677.5 185.2 %all-reduce.10.cloned.1.call-done = (f32[512,1024]{1,0:T(8,128)}, f32[512,1024]{1,0:T(8,128)}) async-done(((f32[512,1024]{1,0:T(8,128)}, f32[512,1024]{1,0:T(8,128)}), (f32[512,1024]{1,0:T(8,128)}, f32[512,1024]{1,0:T(8,128)})) %all-reduce.10.cloned.1.call-update) | async-done | bytes 4194320 | tf_op jit(solution)/shard_map/psum | solution.py:12
  862.7 2.5 multiply_reduce_fusion
  865.2 67.8 %all-reduce = (f32[512]{0:T(512)S(1)}, f32[512]{0:T(512)S(1)}) all-reduce(f32[512]{0:T(512)S(1)} %broadcast_select_fusion.2, f32[512]{0:T(512)S(1)} %broadcast_select_fusion.1), channel_id=1, replica_groups=mesh['row'=16,'col'=8] {'row','col'}, use_global_device_ids=true, to_apply=%region_2.3 | all-reduce | flops 1024 | bytes 8192 | tf_op jit(solution)/shard_map/psum | solution.py:53
  933.0 0.6 sqrt_add_fusion
  (5 shorter events, 0.0 us)
Async XLA Ops:
  7.2 4.4 copy-start
  7.2 99.8 %all-gather.2.cloned.1.call-start = ((), (), s32[]{:S(2)}) async-start(), calls=%async_computation | async-start | bytes 17825792 | tf_op jit(solution)/shard_map/all_gather | solution.py:27
  11.5 227.2 %all-reduce.8.cloned.1.call-start = ((), (), s32[]{:S(2)}) async-start(), calls=%async_computation.2 | async-start | bytes 8388608 | tf_op jit(solution)/shard_map/psum | solution.py:40
  16.1 569.2 %all-reduce.6.cloned.1.call-start = ((), (), s32[]{:S(2)}) async-start(), calls=%async_computation.1 | async-start | bytes 16777216 | tf_op jit(solution)/shard_map/psum | solution.py:12
  115.7 469.7 %copy-start.3 = (f32[2048]{0:T(1024)S(1)}, f32[2048]{0:T(1024)}, u32[]{:S(2)}) copy-start(f32[2048]{0:T(1024)} %param.8) | copy-start | bytes 24580
  115.7 747.0 %all-reduce.10.cloned.1.call-start = ((), (), s32[]{:S(2)}) async-start(), calls=%async_computation.3 | async-start | bytes 8388608 | tf_op jit(solution)/shard_map/psum | solution.py:12
  585.3 71.1 %copy-start.1 = (f32[512,2048]{1,0:T(8,128)S(1)}, f32[512,2048]{1,0:T(8,128)}, u32[]{:S(2)}) copy-start(f32[512,2048]{1,0:T(8,128)} %all-reduce.8.cloned.1.call-done) | copy-start | bytes 12582916
  653.1 3.4 copy-start.4
  656.5 15.3 %copy-start.2 = (f32[2048]{0:T(1024)S(1)}, f32[2048]{0:T(1024)}, u32[]{:S(2)}) copy-start(f32[2048]{0:T(1024)} %param.11) | copy-start | bytes 24580
Sparse Core Ops, SparseCore 0:
  11.7 95.2 all-gather.1
  109.5 129.1 all-reduce.7
  241.8 343.4 all-reduce.5
  671.8 190.8 all-reduce.9
where the time goes:
time: 944 us; the launch traced here: 940 us
  waiting for transfers between devices  742 us (79%)
  matrix products  93.2 us (10%)
  blocking collectives  67.8 us (7%)
  other arithmetic  18 us (2%)
  between operations  14.1 us (1%)
    psum x2, waiting for transfers between devices, spread(): return lax.psum(kept, axis)  529 us
    psum x1, waiting for transfers between devices, body(): cand_col = lax.psum(picked, 'row')  123 us
    all_gather x1, waiting for transfers between devices, body(): col_all = lax.all_gather(masked, 'row', axis=0, tiled=True)  90.8 us
    psum x1, blocking collectives, body(): quad_all, linear_all = lax.psum((quad, linear), ('row', 'col'))  67.8 us
    dot_general x1, matrix products, body(): lax.dot_general(row_all, col_all, contract, precision=high, preferred_ele...  67.7 us
  transfers between devices with their start and end apart: 4, of which 4 were waited for; matrix products, arithmetic and copies ran while one was open for 2% of the time, Pallas kernels for 0%

commit v1 on v0

--- a/solution.py
+++ b/solution.py
@@ -24,7 +24,9 @@
     offset = row_pos % ratio * width_row
     root = row_pos // ratio
     contract = (((0,), (0,)), ((), ()))
-    col_all = lax.all_gather(masked, "row", axis=0, tiled=True)
+    col_all = jnp.concatenate(
+        lax.all_to_all(jnp.stack([masked] * lax.axis_size("row")), "row", 0, 0), axis=0
+    )
     row_all = spread(lax.dynamic_slice_in_dim(col_all, offset, width_row, 1), "col", root)
     tile = lax.dot_general(
         row_all, col_all, contract, precision=high, preferred_element_type=jnp.float32

time: 944 us -> 986 us (1.044)
  waiting for transfers between devices: 742 us -> 771 us
    all_to_all x0 -> x1, waiting for transfers between devices: none -> 246 us  [body(): lax.all_to_all(jnp.stack([masked] * lax.axis_size('row')), 'row', 0, 0)]
    psum x1, waiting for transfers between devices: 123 us -> 0.02 us  [body(): cand_col = lax.psum(picked, 'row')]
    all_gather x1 -> x0, waiting for transfers between devices: 90.8 us -> none  [body(): col_all = lax.all_gather(masked, 'row', axis=0, tiled=True)]
  transfers between devices with their start and end apart: 4 -> 4, of which waited for: 4 -> 3; matrix products, arithmetic and copies ran while one was open for 2% -> 2% of each run, Pallas kernels for 0% -> 0%
where the time goes in v1:
time: 986 us; the launch traced here: 982 us
  waiting for transfers between devices  771 us (78%)
  matrix products  92.5 us (9%)
  blocking collectives  67.8 us (7%)
  other arithmetic  17 us (2%)
  between operations  14.1 us (1%)
  local copies, waits for them, and re-layouts  12.6 us (1%)
    psum x2, waiting for transfers between devices, spread(): return lax.psum(kept, axis)  525 us
    all_to_all x1, waiting for transfers between devices, body(): lax.all_to_all(jnp.stack([masked] * lax.axis_size('row')), 'row', 0, 0)  246 us
    psum x1, blocking collectives, body(): quad_all, linear_all = lax.psum((quad, linear), ('row', 'col'))  67.8 us
    dot_general x1, matrix products, body(): lax.dot_general(row_all, col_all, contract, precision=high, preferred_ele...  67.7 us
  transfers between devices with their start and end apart: 4, of which 3 were waited for; matrix products, arithmetic and copies ran while one was open for 2% of the time, Pallas kernels for 0%

profile of v1, /device:TPU:1, one launch (start us, length us, event | category | flops | bytes accessed | tf_op | source)
XLA Modules:
  0.0 982.0 jit_solution(4010384806060926025)
XLA Ops:
  7.2 0.0 copy-start
  7.2 1.3 dynamic_slice.9
  8.5 0.6 iota_compare_fusion
  9.1 1.4 broadcast_select_fusion
  10.5 7.9 stack.2
  18.4 0.0 copy-start.4
  18.4 7.3 all-to-all-start
  25.7 0.0 all-reduce.8.cloned.1.call-start
  25.7 0.0 copy-done
  25.7 0.0 copy-done.4
  25.7 3.8 fusion
  29.6 0.0 all-reduce.8.cloned.1.call-update
  29.6 0.0 all-reduce.6.cloned.1.call-start
  29.7 245.6 %all-to-all-done = f32[16,128,2048]{2,1,0:T(8,128)} async-done(((f32[16,128,2048]{2,1,0:T(8,128)}), f32[16,128,2048]{2,1,0:T(8,128)}, u32[]{:S(2)}, u32[]{:S(2)}) %all-to-all-start) | async-done | bytes 16777248 | tf_op jit(solution)/shard_map/all_to_all | solution.py:28
  275.3 8.7 dynamic-slice_select_fusion
  283.9 0.0 copy-start.5
  283.9 0.0 all-reduce.6.cloned.1.call-update
  284.0 0.0 all-reduce.10.cloned.1.call-start
  284.0 0.0 all-reduce.8.cloned.1.call-done
  284.1 3.2 dynamic-slice_select_fusion.1
  287.3 339.7 %all-reduce.6.cloned.1.call-done = f32[2048,1024]{1,0:T(8,128)} async-done(((f32[2048,1024]{1,0:T(8,128)}), f32[2048,1024]{1,0:T(8,128)}) %all-reduce.6.cloned.1.call-update) | async-done | bytes 8388624 | tf_op jit(solution)/shard_map/psum | solution.py:12
  627.0 0.0 copy-done.5
  627.0 0.0 copy-start.2
  627.0 67.7 %select_add_fusion = f32[1024,2048]{1,0:T(8,128)S(1)} fusion(f32[2048]{0:T(1024)S(1)} %copy-done.5, s32[2048]{0:T(1024)S(1)} %iota_add_fusion, s32[1024]{0:T(1024)S(1)} %iota_add_fusion.1, f32[2048,1024]{1,0:T(8,128)} %all-reduce.6.cloned.1.call-done, f32[2048,2048]{1,0:T(8,128)} %bitcast.1), kind=kOutput, calls=%fused_computation | convolution fusion | flops 51545899008 | bytes 33574912 | tf_op jit(solution)/shard_map/dot_general | solution.py:31
  694.7 0.0 copy-start.6
  694.8 3.4 copy-done.6
  698.1 0.0 copy-done.2
  698.2 0.0 copy-start.3
  698.2 0.0 copy-start.1
  698.2 15.2 %fusion.5 = f32[512,1024]{1,0:T(8,128)} fusion(f32[512,2048]{1,0:T(8,128)S(1)} %copy-done.2, f32[1024,2048]{1,0:T(8,128)S(1)} %select_add_fusion), kind=kOutput, calls=%fused_computation.17 | convolution fusion | flops 12884901888 | bytes 14680064 | tf_op jit(solution)/shard_map/dot_general | solution.py:45
  713.4 0.0 all-reduce.10.cloned.1.call-update
  713.4 0.0 copy-done.3
  713.4 5.8 fusion.4
  719.2 185.2 %all-reduce.10.cloned.1.call-done = (f32[512,1024]{1,0:T(8,128)}, f32[512,1024]{1,0:T(8,128)}) async-done(((f32[512,1024]{1,0:T(8,128)}, f32[512,1024]{1,0:T(8,128)}), (f32[512,1024]{1,0:T(8,128)}, f32[512,1024]{1,0:T(8,128)})) %all-reduce.10.cloned.1.call-update) | async-done | bytes 4194320 | tf_op jit(solution)/shard_map/psum | solution.py:12
  904.3 2.5 multiply_reduce_fusion
  906.8 67.8 %all-reduce = (f32[512]{0:T(512)S(1)}, f32[512]{0:T(512)S(1)}) all-reduce(f32[512]{0:T(512)S(1)} %broadcast_select_fusion.2, f32[512]{0:T(512)S(1)} %broadcast_select_fusion.1), channel_id=1, replica_groups=mesh['row'=16,'col'=8] {'row','col'}, use_global_device_ids=true, to_apply=%region_2.3 | all-reduce | flops 1024 | bytes 8192 | tf_op jit(solution)/shard_map/psum | solution.py:55
  974.6 0.6 sqrt_add_fusion
  975.2 0.0 copy-done.1
  (5 shorter events, 0.0 us)
Async XLA Ops:
  7.2 18.6 %copy-start = (f32[64,2048]{1,0:T(8,128)S(1)}, f32[64,2048]{1,0:T(8,128)}, u32[]{:S(2)}) copy-start(f32[64,2048]{1,0:T(8,128)} %param.9) | copy-start | bytes 1572868
  18.4 7.4 copy-start.4
  18.4 256.9 %all-to-all-start = ((f32[16,128,2048]{2,1,0:T(8,128)}), f32[16,128,2048]{2,1,0:T(8,128)}, u32[]{:S(2)}, u32[]{:S(2)}) async-start(f32[16,128,2048]{2,1,0:T(8,128)} %stack.2), calls=%async_computation | async-start | bytes 33554432 | tf_op jit(solution)/shard_map/all_to_all | solution.py:28
  25.7 258.4 %all-reduce.8.cloned.1.call-start = ((), (), s32[]{:S(2)}) async-start(), calls=%async_computation.2 | async-start | bytes 8388608 | tf_op jit(solution)/shard_map/psum | solution.py:42
  29.6 597.4 %all-reduce.6.cloned.1.call-start = ((), (), s32[]{:S(2)}) async-start(), calls=%async_computation.1 | async-start | bytes 16777216 | tf_op jit(solution)/shard_map/psum | solution.py:12
  283.9 343.1 %copy-start.5 = (f32[2048]{0:T(1024)S(1)}, f32[2048]{0:T(1024)}, u32[]{:S(2)}) copy-start(f32[2048]{0:T(1024)} %param.8) | copy-start | bytes 24580
  284.0 620.4 %all-reduce.10.cloned.1.call-start = ((), (), s32[]{:S(2)}) async-start(), calls=%async_computation.3 | async-start | bytes 8388608 | tf_op jit(solution)/shard_map/psum | solution.py:12
  627.0 71.1 %copy-start.2 = (f32[512,2048]{1,0:T(8,128)S(1)}, f32[512,2048]{1,0:T(8,128)}, u32[]{:S(2)}) copy-start(f32[512,2048]{1,0:T(8,128)} %all-reduce.8.cloned.1.call-done) | copy-start | bytes 12582916
  694.7 3.4 copy-start.6
  698.2 15.2 %copy-start.3 = (f32[2048]{0:T(1024)S(1)}, f32[2048]{0:T(1024)}, u32[]{:S(2)}) copy-start(f32[2048]{0:T(1024)} %param.11) | copy-start | bytes 24580
  698.2 277.1 %copy-start.1 = (f32[64,2048]{1,0:T(8,128)S(1)}, f32[64,2048]{1,0:T(8,128)}, u32[]{:S(2)}) copy-start(f32[64,2048]{1,0:T(8,128)} %param.9) | copy-start | bytes 1572868
Sparse Core Ops, SparseCore 0:
  29.7 244.2 all-reduce.7
  284.1 342.8 all-reduce.5
  713.5 190.7 all-reduce.9
